TPU v7x, 32 devices: a whole 2x2x4 slice. The times are simulated.
32 devices in a mesh: cand: 2 (over core), test: 8 (over z, x), feat: 2 (over y).
Axes of the slice: x: 2, y: 2, z: 4, core: 2. Of those that a mesh axis runs over, the one named last changes fastest.
Arguments:
- x_test: float32 [32768, 256], P(('test', 'cand'), 'feat'), may hold values from -6 to 6
- x_cand: float32 [8192, 256], P(('cand', 'test'), 'feat'), may hold values from -6 to 6
- w_self: float32 [256, 256], replicated, may hold values from -0.375 to 0.375
- w_neigh: float32 [256, 256], replicated, may hold values from -1.5 to 1.5
- d_out: float32 [8192, 256], P(('cand', 'test'), 'feat'), may hold values from -6 to 6
- block_row: int32 [2, 8, 512], P('cand', 'test'), may hold values from 0 to 31, as said below
- block_col: int32 [2, 8, 512], P('cand', 'test'), may hold values from 0 to 31, as said below
- block_mask: int32 [2, 8, 512, 16, 128], P('cand', 'test'), may hold values from 0 to 255, as said below
- block_live: int32 [2, 8], P('cand', 'test'), may hold values from 170 to 512, as said below
Outputs:
- output: float32 [8192, 256], P(('cand', 'test'), 'feat')
- grad_w_self: float32 [256, 256], P('feat')
- grad_w_neigh: float32 [256, 256], P('feat')
- grad_x_cand: float32 [8192, 256], P(('cand', 'test'), 'feat')
- grad_x_test: float32 [32768, 256], P(('test', 'cand'), 'feat')
Inputs may be any that keep to these rules, and one draw needn't show every extreme that they name: `block_row`: within one device's list the 512 slots name distinct (row block, column block) positions. `block_col`: within one device's list the 512 slots name distinct (row block, column block) positions. `block_mask`: each word holds 8 bits. `block_live`: some device has all 512 slots live in every draw.
All inputs are finite; a program needn't handle non-finite values.
Results may differ from a plain program's by a relative error of at most 0.0003.
Values sent between devices are 32-bit elements; how exact they have to be, the bound alone decides.
No kernel may reach another device: no remote copies, remote signals or barrier semaphores. Data moves between devices by JAX's collectives and lax.ppermute only.
A program may use at most 64 MiB of HBM per device.

v0:
```python
import math
import jax
import jax.numpy as jnp
from jax import lax
from jax.sharding import PartitionSpec as P

HIGHEST = lax.Precision.HIGHEST


def unpack_masks(packed):
    shifts = jnp.arange(8, dtype=jnp.int32)
    bit_cube = jnp.bitwise_and(jnp.right_shift(packed[..., :, None, :], shifts[:, None]), 1)
    return bit_cube.reshape(packed.shape[:-2] + (packed.shape[-2] * 8, packed.shape[-1])).astype(
        jnp.float32
    )


def slot_loop(live_count, offset, stride, slot_total, step_fn, initial):
    group_size = 16
    usable = (live_count - offset + stride - 1) // stride
    group_count = (usable + group_size - 1) // group_size

    def one_group(group_index, running):
        raw_slots = offset + stride * (
            group_index * group_size + jnp.arange(group_size, dtype=jnp.int32)
        )
        weights = (raw_slots < live_count).astype(jnp.float32)
        safe_slots = jnp.minimum(raw_slots, slot_total - 1)
        return step_fn(running, safe_slots, weights)

    return lax.fori_loop(0, group_count, one_group, initial)


def aggregate(
    packed_masks,
    block_rows,
    block_cols,
    live_count,
    offset,
    stride,
    fetch_tiles,
    row_blocks,
    feature_count,
):
    block_edge = packed_masks.shape[-1]

    def step_fn(running, safe_slots, weights):
        row_totals, row_counts = running
        dense_masks = unpack_masks(packed_masks[safe_slots])
        feature_tiles = fetch_tiles(block_cols[safe_slots])
        products = jnp.einsum("gij,gjh->gih", dense_masks, feature_tiles, precision=HIGHEST)
        selector = (
            block_rows[safe_slots][:, None] == jnp.arange(row_blocks, dtype=jnp.int32)[None, :]
        ).astype(jnp.float32) * weights[:, None]
        row_totals = row_totals + jnp.einsum("gk,gih->kih", selector, products, precision=HIGHEST)
        row_counts = row_counts + jnp.einsum(
            "gk,gi->ki", selector, jnp.sum(dense_masks, axis=2), precision=HIGHEST
        )
        return (row_totals, row_counts)

    initial = (
        jnp.zeros((row_blocks, block_edge, feature_count), jnp.float32),
        jnp.zeros((row_blocks, block_edge), jnp.float32),
    )
    return slot_loop(live_count, offset, stride, packed_masks.shape[0], step_fn, initial)


def transpose_product(packed_masks, block_rows, block_cols, live_count, gradient_tiles, col_blocks):
    block_edge = packed_masks.shape[-1]

    def step_fn(running, safe_slots, weights):
        dense_masks = unpack_masks(packed_masks[safe_slots])
        picked = gradient_tiles[block_rows[safe_slots]]
        products = jnp.einsum("gji,gjh->gih", dense_masks, picked, precision=HIGHEST)
        selector = (
            block_cols[safe_slots][:, None] == jnp.arange(col_blocks, dtype=jnp.int32)[None, :]
        ).astype(jnp.float32) * weights[:, None]
        return running + jnp.einsum("gk,gih->kih", selector, products, precision=HIGHEST)

    initial = jnp.zeros((col_blocks, block_edge, gradient_tiles.shape[-1]), jnp.float32)
    return slot_loop(live_count, 0, 1, packed_masks.shape[0], step_fn, initial)


def local(x_test, x_cand, w_self, w_neigh, d_out, block_row, block_col, block_mask, block_live):
    packed_masks = block_mask.reshape(block_mask.shape[2:])
    block_rows = block_row.reshape(-1)
    block_cols = block_col.reshape(-1)
    live_count = block_live.reshape(())
    block_edge = packed_masks.shape[-1]
    cand_count = lax.axis_size("cand")
    test_count = lax.axis_size("test")
    feat_index = lax.axis_index("feat")
    half_width = x_cand.shape[1]
    row_blocks = x_cand.shape[0] * test_count // block_edge
    col_blocks = x_test.shape[0] * cand_count // block_edge
    panel = lax.all_gather(x_test, "cand", axis=0, tiled=True)
    feature_tiles = panel.reshape(col_blocks, block_edge, half_width)

    def fetch_tiles(chosen):
        return feature_tiles[chosen]

    row_totals, row_counts = aggregate(
        packed_masks, block_rows, block_cols, live_count, 0, 1, fetch_tiles, row_blocks, half_width
    )
    own_totals, degree = (
        lax.psum_scatter(
            row_totals.reshape(-1, half_width), "test", scatter_dimension=0, tiled=True
        ),
        lax.psum_scatter(row_counts.reshape(-1), "test", scatter_dimension=0, tiled=True),
    )
    aggregated = own_totals / (1.0 + degree)[:, None]
    self_cols = lax.dynamic_slice_in_dim(w_self, feat_index * half_width, half_width, 1)
    neigh_cols = lax.dynamic_slice_in_dim(w_neigh, feat_index * half_width, half_width, 1)
    self_rows = lax.dynamic_slice_in_dim(w_self, feat_index * half_width, half_width, 0)
    neigh_rows = lax.dynamic_slice_in_dim(w_neigh, feat_index * half_width, half_width, 0)
    cand_full, aggregated_full = (
        lax.all_gather(x_cand, "feat", axis=1, tiled=True),
        lax.all_gather(aggregated, "feat", axis=1, tiled=True),
    )
    pre_act = jnp.dot(cand_full, self_cols, precision=HIGHEST) + jnp.dot(
        aggregated_full, neigh_cols, precision=HIGHEST
    )
    output = jax.nn.silu(pre_act)
    sigmoid_z = jax.nn.sigmoid(pre_act)
    grad_pre = d_out * (sigmoid_z * (1.0 + pre_act * (1.0 - sigmoid_z)))
    grad_full = lax.all_gather(grad_pre, "feat", axis=1, tiled=True)
    self_part = jnp.einsum("rk,rh->kh", x_cand, grad_full, precision=HIGHEST)
    neigh_part = jnp.einsum("rk,rh->kh", aggregated, grad_full, precision=HIGHEST)
    self_sum, neigh_sum = lax.psum((self_part, neigh_part), ("cand", "test"))
    root_count = math.sqrt(x_cand.shape[0] * cand_count * test_count)
    grad_w_self = self_sum / root_count
    grad_w_neigh = neigh_sum / root_count
    grad_x_cand = jnp.dot(grad_full, self_rows.T, precision=HIGHEST)
    grad_agg = jnp.dot(grad_full, neigh_rows.T, precision=HIGHEST)
    lifted = grad_agg / (1.0 + degree)[:, None]
    gathered_rows = lax.all_gather(lifted, "test", axis=0, tiled=True)
    gradient_tiles = gathered_rows.reshape(row_blocks, block_edge, half_width)
    column_terms = transpose_product(
        packed_masks, block_rows, block_cols, live_count, gradient_tiles, col_blocks
    )
    grad_x_test = lax.psum_scatter(
        column_terms.reshape(-1, half_width), "cand", scatter_dimension=0, tiled=True
    )
    return (output, grad_w_self, grad_w_neigh, grad_x_cand, grad_x_test)


def solution(mesh):
    return jax.shard_map(
        local,
        mesh=mesh,
        in_specs=(
            P(("test", "cand"), "feat"),
            P(("cand", "test"), "feat"),
            P(),
            P(),
            P(("cand", "test"), "feat"),
            P("cand", "test", None),
            P("cand", "test", None),
            P("cand", "test", None, None, None),
            P("cand", "test"),
        ),
        out_specs=(
            P(("cand", "test"), "feat"),
            P("feat", None),
            P("feat", None),
            P(("cand", "test"), "feat"),
            P(("test", "cand"), "feat"),
        ),
        check_vma=False,
    )
```

profile of v0, /device:TPU:0, one launch (start us, length us, event | category | flops | bytes accessed | tf_op | source)
XLA Modules:
  0.0 1031.7 jit_solution(8891889499213554505)
XLA Ops:
  8.6 14.2 %all-gather.3.cloned.1.call-done = f32[4096,128]{1,0:T(8,128)} async-done(((f32[2048,128]{1,0:T(8,128)}), f32[4096,128]{1,0:T(8,128)}) %all-gather.3.cloned.1.call-update) | async-done | bytes 2097168 | tf_op jit(solution)/shard_map/all_gather | solution.py:96
  23.8 148.9 %while.22 = (s32[]{:T(128)}, f32[32,128,128]{2,0,1:T(8,128)S(1)}, f32[32,128]{1,0:T(8,128)}, s32[]{:T(128)}, s32[512]{0:T(512)S(1)}, /*index=5*/s32[]{:T(128)}, ...) while((s32[]{:T(128)}, f32[32,128,128]{2,0,1:T(8,128)S(1)}, ...), condition=%wide.region_2.3_spmd, body=%wide.region_0.2_spmd.sunk | while | flops 506468544 | bytes 10039669 | solution.py:31
  25.9 2.7 gather_fusion.2
  34.4 2.9 convolution_add_fusion.7
  39.5 2.7 gather_fusion.2
  47.9 2.9 convolution_add_fusion.7
  53.0 2.7 gather_fusion.2
  61.5 2.9 convolution_add_fusion.7
  66.5 2.7 gather_fusion.2
  75.0 2.9 convolution_add_fusion.7
  80.1 2.7 gather_fusion.2
  88.6 2.9 convolution_add_fusion.7
  93.6 2.7 gather_fusion.2
  102.1 2.9 convolution_add_fusion.7
  107.2 2.7 gather_fusion.2
  115.6 2.9 convolution_add_fusion.7
  120.7 2.7 gather_fusion.2
  129.2 2.9 convolution_add_fusion.7
  134.2 2.7 gather_fusion.2
  142.7 2.9 convolution_add_fusion.7
  147.8 2.7 gather_fusion.2
  156.2 2.9 convolution_add_fusion.7
  161.3 2.7 gather_fusion.2
  169.8 2.9 convolution_add_fusion.7
  172.7 2.5 copy.56
  177.6 9.2 all_gather.15
  187.5 321.7 %all-reduce = f32[4096]{0:T(1024)S(1)} all-reduce(f32[4096]{0:T(1024)} %bitcast.18), channel_id=3, replica_groups=mesh['cand'=2,'test'=8,'feat'=2] {'test'}, use_global_device_ids=true, to_apply=%region_4.5.clone | all-reduce | flops 4096 | bytes 32768
  509.3 20.2 %reduce-scatter.3.cloned.1.call-done = f32[512,128]{1,0:T(8,128)} async-done(((f32[4096,128]{1,0:T(8,128)}), f32[512,128]{1,0:T(8,128)}) %reduce-scatter.3.cloned.1.call-update) | async-done | bytes 262160 | tf_op jit(solution)/shard_map/reduce_scatter | solution.py:106
  530.6 7.2 all_gather.17
  539.2 7.0 all_gather.18
  550.6 45.6 %all-gather.5.cloned.1.call-done = f32[4096,128]{1,0:T(8,128)} async-done(((f32[512,128]{1,0:T(8,128)}), f32[4096,128]{1,0:T(8,128)}) %all-gather.5.cloned.1.call-update) | async-done | bytes 2097168 | tf_op jit(solution)/shard_map/all_gather | solution.py:136
  596.5 143.8 %while.23 = (s32[]{:T(128)}, f32[32,128,128]{2,0,1:T(8,128)S(1)}, s32[]{:T(128)}, s32[512]{0:T(512)S(1)}, s32[]{:T(128)}, /*index=5*/s32[512,16,128]{2,1,0:T(8,1...) while((s32[]{:T(128)}, f32[32,128,128]{2,0,1:T(8,128)S(1)}, s32[]{:T(128)}, ...), condition=%wide.region_8.9_spmd, body=%wide.region_7.8_spmd.sunk | while | flops 504630464 | bytes 9842357 | solution.py:31
  599.8 2.7 gather_fusion.6
  602.6 2.2 gather_fusion.5
  606.8 2.9 convolution_add_fusion.9
  612.9 2.8 gather_fusion.6
  615.6 2.2 gather_fusion.5
  619.9 2.9 convolution_add_fusion.9
  625.9 2.8 gather_fusion.6
  632.9 2.9 convolution_add_fusion.9
  639.0 2.8 gather_fusion.6
  641.7 2.2 gather_fusion.5
  646.0 2.9 convolution_add_fusion.9
  652.0 2.7 gather_fusion.6
  659.0 2.9 convolution_add_fusion.9
  665.1 2.8 gather_fusion.6
  667.9 2.2 gather_fusion.5
  672.1 2.9 convolution_add_fusion.9
  678.2 2.8 gather_fusion.6
  680.9 2.2 gather_fusion.5
  685.2 2.9 convolution_add_fusion.9
  691.2 2.7 gather_fusion.6
  694.0 2.2 gather_fusion.5
  698.2 2.9 convolution_add_fusion.9
  704.3 2.7 gather_fusion.6
  707.0 2.2 gather_fusion.5
  711.2 2.9 convolution_add_fusion.9
  717.3 2.7 gather_fusion.6
  720.1 2.2 gather_fusion.5
  724.3 2.9 convolution_add_fusion.9
  730.4 2.7 gather_fusion.6
  737.3 2.9 convolution_add_fusion.9
  740.2 2.5 copy.60
  748.8 276.4 %reduce-scatter.5.cloned.1.call-done = f32[2048,128]{1,0:T(8,128)} async-done(((f32[4096,128]{1,0:T(8,128)}), f32[2048,128]{1,0:T(8,128)}) %reduce-scatter.5.cloned.1.call-update) | async-done | bytes 1048592 | tf_op jit(solution)/shard_map/reduce_scatter | solution.py:141
  (449 shorter events, 165.5 us)
Async XLA Ops:
  7.2 530.6 %copy-start = (f32[256,256]{1,0:T(8,128)S(1)}, f32[256,256]{1,0:T(8,128)}, u32[]{:S(2)}) copy-start(f32[256,256]{1,0:T(8,128)} %param.16) | copy-start | bytes 786436
  7.2 16.6 %copy-start.2 = (s32[1,1,512]{2,1,0:T(1,128)S(1)}, s32[1,1,512]{2,1,0:T(1,128)}, u32[]{:S(2)}) copy-start(s32[1,1,512]{2,1,0:T(1,128)} %param.19) | copy-start | bytes 6148
  7.2 16.6 %copy-start.1 = (s32[1,1,512]{2,1,0:T(1,128)S(1)}, s32[1,1,512]{2,1,0:T(1,128)}, u32[]{:S(2)}) copy-start(s32[1,1,512]{2,1,0:T(1,128)} %param.18) | copy-start | bytes 6148
  7.2 15.7 %all-gather.3.cloned.1.call-start = ((), (), s32[]{:S(2)}) async-start(), calls=%async_computation.2 | async-start | bytes 3145728 | tf_op jit(solution)/shard_map/all_gather | solution.py:96
  7.9 521.5 %reduce-scatter.3.cloned.1.call-start = ((), (), s32[]{:S(2)}) async-start(), calls=%async_computation.3 | async-start | bytes 2359296 | tf_op jit(solution)/shard_map/reduce_scatter | solution.py:106
  24.4 4.7 copy-start.13
  25.2 4.0 copy-start.10
  33.0 1.4 copy-start.11
  38.0 4.7 copy-start.13
  38.7 4.0 copy-start.10
  46.6 1.4 copy-start.11
  51.5 4.7 copy-start.13
  52.2 4.0 copy-start.10
  65.1 4.7 copy-start.13
  65.8 4.0 copy-start.10
  73.6 1.4 copy-start.11
  78.6 4.7 copy-start.13
  79.3 4.0 copy-start.10
  92.1 4.7 copy-start.13
  92.8 4.0 copy-start.10
  100.7 1.4 copy-start.11
  105.7 4.7 copy-start.13
  106.4 4.0 copy-start.10
  114.3 1.4 copy-start.11
  119.2 4.7 copy-start.13
  119.9 4.0 copy-start.10
  127.8 1.4 copy-start.11
  132.7 4.7 copy-start.13
  133.4 4.0 copy-start.10
  146.3 4.7 copy-start.13
  147.0 4.0 copy-start.10
  154.9 1.4 copy-start.11
  159.8 4.7 copy-start.13
  160.5 4.0 copy-start.10
  175.2 2.3 copy-start.5
  175.2 11.5 %copy-start.7 = (f32[256,256]{1,0:T(8,128)S(1)}, f32[256,256]{1,0:T(8,128)}, u32[]{:S(2)}) copy-start(f32[256,256]{1,0:T(8,128)} %param.15) | copy-start | bytes 786436
  175.3 420.9 %all-gather.5.cloned.1.call-start = ((), (), s32[]{:S(2)}) async-start(), calls=%async_computation.4 | async-start | bytes 2359296 | tf_op jit(solution)/shard_map/all_gather | solution.py:136
  546.2 50.0 %copy-start.3 = (f32[512,256]{0,1:T(8,128)}, f32[512,256]{0,1:T(8,128)S(1)}, u32[]{:S(2)}) copy-start(f32[512,256]{0,1:T(8,128)S(1)} %all_gather.18) | copy-start | bytes 1572868
  548.0 198.3 %all-reduce.4.cloned.1.call-start = ((), (), s32[]{:S(2)}) async-start(), calls=%async_computation.6 | async-start | bytes 524288 | tf_op jit(solution)/shard_map/psum | solution.py:129
  550.5 474.6 %reduce-scatter.5.cloned.1.call-start = ((), (), s32[]{:S(2)}) async-start(), calls=%async_computation.5 | async-start | bytes 3145728 | tf_op jit(solution)/shard_map/reduce_scatter | solution.py:141
  604.8 2.0 copy-start.12
  604.8 2.0 copy-start.15
  617.8 2.0 copy-start.12
  617.9 2.0 copy-start.15
  630.9 2.0 copy-start.12
  630.9 2.0 copy-start.15
  644.0 2.0 copy-start.12
  644.0 2.0 copy-start.15
  657.0 2.0 copy-start.12
  657.0 2.0 copy-start.15
  670.1 2.0 copy-start.12
  670.1 2.0 copy-start.15
  683.1 2.0 copy-start.12
  683.2 2.0 copy-start.15
  696.2 2.0 copy-start.12
  696.2 2.0 copy-start.15
  709.2 2.0 copy-start.12
  709.2 2.0 copy-start.15
  722.3 2.0 copy-start.12
  722.3 2.0 copy-start.15
  735.3 2.0 copy-start.12
  735.3 2.0 copy-start.15
  742.8 1.8 copy-start.4
  742.8 1.8 copy-start.8
  (18 other events, 23.3 us)
Sparse Core Ops, SparseCore 0:
  9.6 13.2 all-gather.2
  175.4 354.0 reduce-scatter.2
  548.1 48.0 all-gather.4
  600.1 88.4 all-reduce.3
  742.9 282.1 reduce-scatter.4
where the time goes:
time: 1040 us; the launch traced here: 1030 us
  waiting for transfers between devices  357 us (34%)
  blocking collectives  345 us (33%)
  local copies, waits for them, and re-layouts  159 us (15%)
  matrix products  126 us (12%)
  other arithmetic  26.6 us (3%)
  between operations  15.2 us (1%)
    unnamed x1, blocking collectives  322 us
    reduce_scatter x1, waiting for transfers between devices, local(): lax.psum_scatter(column_terms.reshape(-1, half_width), 'cand', scatter_di...  276 us
    dot_general x22, matrix products, step_fn(): jnp.einsum('gk,gih->kih', selector, products, precision=HIGHEST)  63.6 us
    gather x22, local copies, waits for them, and re-layouts, step_fn(): dense_masks = unpack_masks(packed_masks[safe_slots])  60.5 us
    all_gather x1, waiting for transfers between devices, local(): gathered_rows = lax.all_gather(lifted, 'test', axis=0, tiled=True)  45.6 us
    gather x22, local copies, waits for them, and re-layouts, step_fn(): picked = gradient_tiles[block_rows[safe_slots]]  31.6 us
    gather x11, local copies, waits for them, and re-layouts, fetch_tiles(): return feature_tiles[chosen]  24.2 us
    dot_general x11, matrix products, step_fn(): jnp.einsum('gji,gjh->gih', dense_masks, picked, precision=HIGHEST)  21.6 us
  transfers between devices with their start and end apart: 5, of which 4 were waited for; matrix products, arithmetic and copies ran while one was open for 15% of the time, Pallas kernels for 0%

commit v1 on v0

--- a/solution.py
+++ b/solution.py
@@ -133,7 +133,24 @@
     grad_x_cand = jnp.dot(grad_full, self_rows.T, precision=HIGHEST)
     grad_agg = jnp.dot(grad_full, neigh_rows.T, precision=HIGHEST)
     lifted = grad_agg / (1.0 + degree)[:, None]
-    gathered_rows = lax.all_gather(lifted, "test", axis=0, tiled=True)
+    peers, place, rows = (lax.axis_size("test"), lax.axis_index("test"), lifted.shape[0])
+    right = [(i, (i + 1) % peers) for i in range(peers)]
+    backward = [(i, (i - 1) % peers) for i in range(peers)]
+    whole = jnp.zeros((*lifted.shape[:0], peers * rows, *lifted.shape[0 + 1 :]), lifted.dtype)
+    whole = lax.dynamic_update_slice_in_dim(whole, lifted, place * rows, axis=0)
+    from_left = from_right = lifted
+    half = peers // 2
+    for step in range(1, half + 1):
+        from_left = lax.ppermute(from_left, "test", right)
+        whole = lax.dynamic_update_slice_in_dim(
+            whole, from_left, (place - step) % peers * rows, axis=0
+        )
+        if step < peers - half:
+            from_right = lax.ppermute(from_right, "test", backward)
+            whole = lax.dynamic_update_slice_in_dim(
+                whole, from_right, (place + step) % peers * rows, axis=0
+            )
+    gathered_rows = whole
     gradient_tiles = gathered_rows.reshape(row_blocks, block_edge, half_width)
     column_terms = transpose_product(
         packed_masks, block_rows, block_cols, live_count, gradient_tiles, col_blocks

time: 1040 us -> 1040 us (level)
  waiting for transfers between devices: 357 us -> 337 us
  starting transfers between devices: 0.2 us -> 18 us
    all_gather x1 -> x0, waiting for transfers between devices: 45.6 us -> none  [local(): gathered_rows = lax.all_gather(lifted, 'test', axis=0, tiled=True)]
    ppermute x0 -> x7, waiting for transfers between devices: none -> 25.1 us  [the longest x4 23.4 us: local(): from_left = lax.ppermute(from_left, 'test', right)]
    ppermute x0 -> x7, starting transfers between devices: none -> 17.8 us  [the longest x3 9.61 us: local(): from_right = lax.ppermute(from_right, 'test', backward)]
  transfers between devices with their start and end apart: 5 -> 11, of which waited for: 4 -> 9; matrix products, arithmetic and copies ran while one was open for 15% -> 15% of each run, Pallas kernels for 0% -> 0%
where the time goes in v1:
time: 1040 us; the launch traced here: 1030 us
  blocking collectives  345 us (33%)
  waiting for transfers between devices  337 us (32%)
  local copies, waits for them, and re-layouts  164 us (16%)
  matrix products  126 us (12%)
  other arithmetic  26.6 us (3%)
  starting transfers between devices  18 us (2%)
  between operations  15.3 us (1%)
    unnamed x1, blocking collectives  322 us
    reduce_scatter x1, waiting for transfers between devices, local(): lax.psum_scatter(column_terms.reshape(-1, half_width), 'cand', scatter_di...  277 us
    dot_general x22, matrix products, step_fn(): jnp.einsum('gk,gih->kih', selector, products, precision=HIGHEST)  63.6 us
    gather x22, local copies, waits for them, and re-layouts, step_fn(): dense_masks = unpack_masks(packed_masks[safe_slots])  60.5 us
    gather x22, local copies, waits for them, and re-layouts, step_fn(): picked = gradient_tiles[block_rows[safe_slots]]  31.6 us
    gather x11, local copies, waits for them, and re-layouts, fetch_tiles(): return feature_tiles[chosen]  24.2 us
    ppermute x4, waiting for transfers between devices, local(): from_left = lax.ppermute(from_left, 'test', right)  23.4 us
    dot_general x11, matrix products, step_fn(): jnp.einsum('gji,gjh->gih', dense_masks, picked, precision=HIGHEST)  21.8 us
  transfers between devices with their start and end apart: 11, of which 9 were waited for; matrix products, arithmetic and copies ran while one was open for 15% of the time, Pallas kernels for 0%

profile of v1, /device:TPU:0, one launch (start us, length us, event | category | flops | bytes accessed | tf_op | source)
XLA Modules:
  0.0 1034.2 jit_solution(5243089789748248349)
XLA Ops:
  8.6 14.2 %all-gather.2.cloned.1.call-done = f32[4096,128]{1,0:T(8,128)} async-done(((f32[2048,128]{1,0:T(8,128)}), f32[4096,128]{1,0:T(8,128)}) %all-gather.2.cloned.1.call-update) | async-done | bytes 2097168 | tf_op jit(solution)/shard_map/all_gather | solution.py:96
  23.8 149.0 %while.22 = (s32[]{:T(128)}, f32[32,128,128]{2,0,1:T(8,128)S(1)}, f32[32,128]{1,0:T(8,128)}, s32[]{:T(128)}, s32[512]{0:T(512)S(1)}, /*index=5*/s32[]{:T(128)}, ...) while((s32[]{:T(128)}, f32[32,128,128]{2,0,1:T(8,128)S(1)}, ...), condition=%wide.region_2.3_spmd, body=%wide.region_0.2_spmd.sunk | while | flops 506468544 | bytes 10039669 | solution.py:31
  25.9 2.7 gather_fusion.2
  34.4 2.9 convolution_add_fusion.7
  39.5 2.7 gather_fusion.2
  48.0 2.9 convolution_add_fusion.7
  53.0 2.7 gather_fusion.2
  61.5 2.9 convolution_add_fusion.7
  66.6 2.7 gather_fusion.2
  75.1 2.9 convolution_add_fusion.7
  80.1 2.7 gather_fusion.2
  88.6 2.9 convolution_add_fusion.7
  93.7 2.7 gather_fusion.2
  102.2 2.9 convolution_add_fusion.7
  107.2 2.7 gather_fusion.2
  115.7 2.9 convolution_add_fusion.7
  120.8 2.7 gather_fusion.2
  129.3 2.9 convolution_add_fusion.7
  134.3 2.7 gather_fusion.2
  142.8 2.9 convolution_add_fusion.7
  147.9 2.7 gather_fusion.2
  156.4 2.9 convolution_add_fusion.7
  161.4 2.7 gather_fusion.2
  169.9 2.9 convolution_add_fusion.7
  172.8 2.6 copy.56
  177.7 9.2 all_gather.12
  187.6 322.0 %all-reduce = f32[4096]{0:T(1024)S(1)} all-reduce(f32[4096]{0:T(1024)} %bitcast.18), channel_id=3, replica_groups=mesh['cand'=2,'test'=8,'feat'=2] {'test'}, use_global_device_ids=true, to_apply=%region_4.5.clone | all-reduce | flops 4096 | bytes 32768
  509.7 19.9 %reduce-scatter.3.cloned.1.call-done = f32[512,128]{1,0:T(8,128)} async-done(((f32[4096,128]{1,0:T(8,128)}), f32[512,128]{1,0:T(8,128)}) %reduce-scatter.3.cloned.1.call-update) | async-done | bytes 262160 | tf_op jit(solution)/shard_map/reduce_scatter | solution.py:106
  530.7 7.2 all_gather.14
  539.4 7.0 all_gather.15
  549.1 3.9 collective-permute-start.1
  553.0 5.9 collective-permute-done
  558.9 2.5 collective-permute-start.2
  563.5 2.9 collective-permute-start.3
  567.7 5.3 collective-permute-done.2
  573.0 2.5 collective-permute-start.4
  578.3 2.8 collective-permute-start.5
  582.1 5.3 collective-permute-done.4
  589.9 6.9 collective-permute-done.6
  598.4 144.1 %while.23 = (s32[]{:T(128)}, f32[32,128,128]{2,0,1:T(8,128)S(1)}, s32[]{:T(128)}, s32[512]{0:T(512)S(1)}, s32[]{:T(128)}, /*index=5*/s32[512,16,128]{2,1,0:T(8,1...) while((s32[]{:T(128)}, f32[32,128,128]{2,0,1:T(8,128)S(1)}, s32[]{:T(128)}, ...), condition=%wide.region_8.9_spmd, body=%wide.region_7.8_spmd.sunk | while | flops 504630464 | bytes 9842357 | solution.py:31
  601.6 2.8 gather_fusion.6
  608.6 2.9 convolution_add_fusion.9
  614.7 2.8 gather_fusion.6
  621.7 2.9 convolution_add_fusion.9
  627.8 2.7 gather_fusion.6
  634.8 2.9 convolution_add_fusion.9
  640.9 2.8 gather_fusion.6
  647.9 2.9 convolution_add_fusion.9
  654.0 2.8 gather_fusion.6
  661.0 2.9 convolution_add_fusion.9
  667.1 2.7 gather_fusion.6
  674.1 2.9 convolution_add_fusion.9
  680.2 2.7 gather_fusion.6
  687.2 2.9 convolution_add_fusion.9
  693.3 2.7 gather_fusion.6
  700.3 2.9 convolution_add_fusion.9
  706.4 2.7 gather_fusion.6
  713.4 2.9 convolution_add_fusion.9
  719.5 2.7 gather_fusion.6
  726.5 2.9 convolution_add_fusion.9
  732.6 2.7 gather_fusion.6
  739.6 2.9 convolution_add_fusion.9
  742.5 2.6 copy.60
  751.1 276.6 %reduce-scatter.5.cloned.1.call-done = f32[2048,128]{1,0:T(8,128)} async-done(((f32[4096,128]{1,0:T(8,128)}), f32[2048,128]{1,0:T(8,128)}) %reduce-scatter.5.cloned.1.call-update) | async-done | bytes 1048592 | tf_op jit(solution)/shard_map/reduce_scatter | solution.py:158
  (470 shorter events, 193.1 us)
Async XLA Ops:
  7.2 530.7 %copy-start = (f32[256,256]{1,0:T(8,128)S(1)}, f32[256,256]{1,0:T(8,128)}, u32[]{:S(2)}) copy-start(f32[256,256]{1,0:T(8,128)} %param.16) | copy-start | bytes 786436
  7.2 16.6 %copy-start.2 = (s32[1,1,512]{2,1,0:T(1,128)S(1)}, s32[1,1,512]{2,1,0:T(1,128)}, u32[]{:S(2)}) copy-start(s32[1,1,512]{2,1,0:T(1,128)} %param.19) | copy-start | bytes 6148
  7.2 16.6 %copy-start.1 = (s32[1,1,512]{2,1,0:T(1,128)S(1)}, s32[1,1,512]{2,1,0:T(1,128)}, u32[]{:S(2)}) copy-start(s32[1,1,512]{2,1,0:T(1,128)} %param.18) | copy-start | bytes 6148
  7.2 15.7 %all-gather.2.cloned.1.call-start = ((), (), s32[]{:S(2)}) async-start(), calls=%async_computation.2 | async-start | bytes 3145728 | tf_op jit(solution)/shard_map/all_gather | solution.py:96
  7.9 521.7 %reduce-scatter.3.cloned.1.call-start = ((), (), s32[]{:S(2)}) async-start(), calls=%async_computation.3 | async-start | bytes 2359296 | tf_op jit(solution)/shard_map/reduce_scatter | solution.py:106
  24.4 4.7 copy-start.14
  25.2 4.0 copy-start.11
  38.0 4.7 copy-start.14
  38.7 4.0 copy-start.11
  51.5 4.7 copy-start.14
  52.2 4.0 copy-start.11
  60.1 1.4 copy-start.12
  65.1 4.7 copy-start.14
  65.8 4.0 copy-start.11
  78.6 4.7 copy-start.14
  79.3 4.0 copy-start.11
  92.2 4.7 copy-start.14
  92.9 4.0 copy-start.11
  105.7 4.7 copy-start.14
  106.4 4.0 copy-start.11
  119.3 4.7 copy-start.14
  120.0 4.0 copy-start.11
  132.8 4.7 copy-start.14
  133.5 4.0 copy-start.11
  146.4 4.7 copy-start.14
  147.1 4.0 copy-start.11
  159.9 4.7 copy-start.14
  160.6 4.0 copy-start.11
  175.4 2.3 copy-start.6
  175.4 11.5 %copy-start.8 = (f32[256,256]{1,0:T(8,128)S(1)}, f32[256,256]{1,0:T(8,128)}, u32[]{:S(2)}) copy-start(f32[256,256]{1,0:T(8,128)} %param.15) | copy-start | bytes 786436
  175.4 573.1 %all-reduce.4.cloned.1.call-start = ((), (), s32[]{:S(2)}) async-start(), calls=%async_computation.5 | async-start | bytes 524288 | tf_op jit(solution)/shard_map/psum | solution.py:129
  546.4 20.0 %copy-start.4 = (f32[512,256]{0,1:T(8,128)}, f32[512,256]{0,1:T(8,128)S(1)}, u32[]{:S(2)}) copy-start(f32[512,256]{0,1:T(8,128)S(1)} %all_gather.15) | copy-start | bytes 1572868
  548.3 10.6 %collective-permute-start = (f32[512,128]{1,0:T(8,128)}, f32[512,128]{1,0:T(8,128)}, u32[]{:S(2)}, u32[]{:S(2)}) collective-permute-start(f32[512,128]{1,0:T(8,128)} %get-tuple-element.164), channel_id=1, source_target_pairs={{0,2},{2,4},{4,6},{6,8},{8,10},{10,12},{12,14},{14,0},{1,3},{3,5},... | collective-permute-start | bytes 786440 | tf_op jit(solution)/shard_map/ppermute | solution.py:144
  549.1 14.3 %collective-permute-start.1 = (f32[512,128]{1,0:T(8,128)}, f32[512,128]{1,0:T(8,128)}, u32[]{:S(2)}, u32[]{:S(2)}) collective-permute-start(f32[512,128]{1,0:T(8,128)} %get-tuple-element.164), channel_id=1, source_target_pairs={{0,14},{2,0},{4,2},{6,4},{8,6},{10,8},{12,10},{14,12},{1,15},{3,1}... | collective-permute-start | bytes 786440 | tf_op jit(solution)/shard_map/ppermute | solution.py:149
  558.9 14.2 %collective-permute-start.2 = (f32[512,128]{1,0:T(8,128)}, f32[512,128]{1,0:T(8,128)}, u32[]{:S(2)}, u32[]{:S(2)}) collective-permute-start(f32[512,128]{1,0:T(8,128)} %collective-permute-done), channel_id=1, source_target_pairs={{0,2},{2,4},{4,6},{6,8},{8,10},{10,12},{12,14},{14,0},{1,3},{3,5},... | collective-permute-start | bytes 786440 | tf_op jit(solution)/shard_map/ppermute | solution.py:144
  563.5 14.8 %collective-permute-start.3 = (f32[512,128]{1,0:T(8,128)}, f32[512,128]{1,0:T(8,128)S(1)}, u32[]{:S(2)}, u32[]{:S(2)}) collective-permute-start(f32[512,128]{1,0:T(8,128)} %collective-permute-done.1), channel_id=1, source_target_pairs={{0,14},{2,0},{4,2},{6,4},{8,6},{10,8},{12,10},{14,12},{1,15},{3,1}... | collective-permute-start | bytes 786440 | tf_op jit(solution)/shard_map/ppermute | solution.py:149
  567.7 460.0 %reduce-scatter.5.cloned.1.call-start = ((), (), s32[]{:S(2)}) async-start(), calls=%async_computation.4 | async-start | bytes 3145728 | tf_op jit(solution)/shard_map/reduce_scatter | solution.py:158
  573.0 14.4 %collective-permute-start.4 = (f32[512,128]{1,0:T(8,128)}, f32[512,128]{1,0:T(8,128)S(1)}, u32[]{:S(2)}, u32[]{:S(2)}) collective-permute-start(f32[512,128]{1,0:T(8,128)} %collective-permute-done.2), channel_id=1, source_target_pairs={{0,2},{2,4},{4,6},{6,8},{8,10},{10,12},{12,14},{14,0},{1,3},{3,5},... | collective-permute-start | bytes 786440 | tf_op jit(solution)/shard_map/ppermute | solution.py:144
  578.3 11.5 %collective-permute-start.5 = (f32[512,128]{1,0:T(8,128)S(1)}, f32[512,128]{1,0:T(8,128)S(1)}, u32[]{:S(2)}, u32[]{:S(2)}) collective-permute-start(f32[512,128]{1,0:T(8,128)S(1)} %collective-permute-done.3), channel_id=1, source_target_pairs={{0,14},{2,0},{4,2},{6,4},{8,6},{10,8},{12,10},{14,12},{1,15},{3,1}... | collective-permute-start | bytes 786440 | tf_op jit(solution)/shard_map/ppermute | solution.py:149
  587.4 9.4 collective-permute-start.6
  606.6 2.0 copy-start.13
  606.6 2.0 copy-start.16
  619.7 2.0 copy-start.13
  619.7 2.0 copy-start.16
  632.8 2.0 copy-start.13
  632.8 2.0 copy-start.16
  645.9 2.0 copy-start.13
  645.9 2.0 copy-start.16
  659.0 2.0 copy-start.13
  659.0 2.0 copy-start.16
  672.1 2.0 copy-start.13
  672.1 2.0 copy-start.16
  685.2 2.0 copy-start.13
  685.2 2.0 copy-start.16
  698.3 2.0 copy-start.13
  698.3 2.0 copy-start.16
  711.4 2.0 copy-start.13
  711.4 2.0 copy-start.16
  724.5 2.0 copy-start.13
  724.5 2.0 copy-start.16
  737.6 2.0 copy-start.13
  737.6 2.0 copy-start.16
  745.0 1.8 copy-start.5
  745.0 1.8 copy-start.9
  (25 other events, 32.9 us)
Sparse Core Ops, SparseCore 0:
  9.6 13.2 all-gather.1
  175.5 354.0 reduce-scatter.2
  567.8 93.5 all-reduce.3
  745.2 282.4 reduce-scatter.4
